TPU v7x, 256 devices: a whole 4x4x8 slice. The times are simulated.
256 devices in a mesh: dp: 16 (over y_lo, z), fsdp: 16 (over x, y_hi, core).
Axes of the slice: x: 4, y: 4 (y_hi: 2, y_lo: 2; y = y_hi * 2 + y_lo), z: 8, core: 2. Of those that a mesh axis runs over, the one named last changes fastest.
Arguments:
- latents: bfloat16 [1024, 8, 8, 640], P(('dp', 'fsdp'))
- bucket: int32 [1024], P(('dp', 'fsdp')), may hold values from 0 to 39
- cotangent: bfloat16 [1024, 4, 4, 640], P(('dp', 'fsdp')), may hold values from -6 to 6
- tile_count: int32 [256], P(('dp', 'fsdp')), may hold values from 1 to 4, as said below
- cond_table: float32 [40, 640], replicated, may hold values from -3 to 3
- norm_gain: float32 [640], replicated, may hold values from 0.1 to 1.9
- norm_shift: float32 [640], replicated, may hold values from -3 to 3
- conv_bias: float32 [640], replicated, may hold values from -3 to 3
- down_bias: float32 [640], replicated, may hold values from -3 to 3
- conv_weight: bfloat16 [5760, 640], P('fsdp'), may hold values from -0.078125 to 0.078125
- down_weight: bfloat16 [5760, 640], P('fsdp'), may hold values from -0.078125 to 0.078125
Outputs:
- block_output: bfloat16 [1024, 4, 4, 640], P(('dp', 'fsdp'))
- grad_input: bfloat16 [1024, 8, 8, 640], P(('dp', 'fsdp'))
- grad_conv: float32 [5760, 640], P('fsdp')
- grad_affine: float32 [3, 640], replicated
Inputs may be any that keep to these rules, and one draw needn't show every extreme that they name: Slots 0 to tile_count - 1 of a device are live; some device holds exactly 4 live tiles.
All inputs are finite; a program needn't handle non-finite values.
Results may differ from a plain program's by a relative error of at most 0.005.
Values may be sent and summed in bfloat16 or wider, within the bound.
No kernel may reach another device: no remote copies, remote signals or barrier semaphores. Data moves between devices by JAX's collectives and lax.ppermute only.
A program may use at most 128 MiB of HBM per device.

v0:
```python
import math

import jax
import jax.numpy as jnp
from jax import lax
from jax.sharding import PartitionSpec as P

GROUPS = 32


def tap_patches(values):
    tile_side = values.shape[1]
    channels = values.shape[3]
    padded = jnp.pad(values, ((0, 0), (1, 1), (1, 1), (0, 0)))
    pieces = [
        padded[:, row_off : row_off + tile_side, col_off : col_off + tile_side, :]
        for row_off in range(3)
        for col_off in range(3)
    ]
    return jnp.concatenate(pieces, axis=-1).reshape(-1, 9 * channels)


def down_patches(values):
    tile_side = values.shape[1]
    channels = values.shape[3]
    padded = jnp.pad(values, ((0, 0), (1, 1), (1, 1), (0, 0)))
    pieces = [
        padded[:, row_off : row_off + tile_side - 1 : 2, col_off : col_off + tile_side - 1 : 2, :]
        for row_off in range(3)
        for col_off in range(3)
    ]
    return jnp.concatenate(pieces, axis=-1).reshape(-1, 9 * channels)


def fold_taps(grads, tile_side, stride):
    tile_total = grads.shape[0]
    channels = grads.shape[3] // 9
    padded = jnp.zeros((tile_total, tile_side + 2, tile_side + 2, channels), jnp.float32)
    for tap_index in range(9):
        row_off = tap_index // 3
        col_off = tap_index % 3
        stop_row = row_off + tile_side - (stride - 1)
        stop_col = col_off + tile_side - (stride - 1)
        padded = padded.at[:, row_off:stop_row:stride, col_off:stop_col:stride, :].add(
            grads[..., tap_index * channels : (tap_index + 1) * channels]
        )
    return padded[:, 1 : tile_side + 1, 1 : tile_side + 1, :]


def group_mean(channel_sums, member, per_group):
    grouped = jnp.dot(channel_sums, member, precision=lax.Precision.HIGHEST) / per_group
    return jnp.dot(grouped, jnp.transpose(member), precision=lax.Precision.HIGHEST)


def tile_pass(latent_block, bucket_block, cotangent_block, params):
    cond_table, norm_gain, norm_shift, conv_bias, down_bias, conv_full, down_full = params
    tile_total = latent_block.shape[0]
    tile_side = latent_block.shape[1]
    channels = latent_block.shape[3]
    half_side = tile_side // 2
    member = (
        jnp.arange(channels, dtype=jnp.int32)[:, None] // (channels // GROUPS)
        == jnp.arange(GROUPS, dtype=jnp.int32)[None, :]
    ).astype(jnp.float32)
    per_group = tile_side * tile_side * (channels // GROUPS)
    values = latent_block.astype(jnp.float32)
    center = group_mean(jnp.sum(values, axis=(1, 2)), member, per_group)
    deviation = values - center[:, None, None, :]
    spread = group_mean(jnp.sum(deviation * deviation, axis=(1, 2)), member, per_group)
    inv_std = lax.rsqrt(spread + 1e-05)[:, None, None, :]
    normed = deviation * inv_std
    pre_act = normed * norm_gain + norm_shift
    sigmoid_v = jax.nn.sigmoid(pre_act)
    activated = (pre_act * sigmoid_v).astype(jnp.bfloat16)
    onehot = (
        bucket_block[:, None] == jnp.arange(cond_table.shape[0], dtype=jnp.int32)[None, :]
    ).astype(jnp.float32)
    conditioning = jnp.dot(onehot, cond_table, precision=lax.Precision.HIGHEST)
    conv_out = jnp.dot(
        tap_patches(activated), conv_full, preferred_element_type=jnp.float32
    ).reshape(tile_total, tile_side, tile_side, channels)
    conv_out = conv_out + conv_bias + conditioning[:, None, None, :]
    residual = (values + conv_out).astype(jnp.bfloat16)
    down_out = jnp.dot(
        down_patches(residual), down_full, preferred_element_type=jnp.float32
    ).reshape(tile_total, half_side, half_side, channels)
    block_output = (down_out + down_bias).astype(jnp.bfloat16)
    back_down = lax.dot_general(
        cotangent_block.reshape(-1, channels),
        down_full,
        (((1,), (1,)), ((), ())),
        preferred_element_type=jnp.float32,
    )
    grad_resid = fold_taps(
        back_down.reshape(tile_total, half_side, half_side, 9 * channels), tile_side, 2
    )
    grad_hidden = grad_resid.astype(jnp.bfloat16)
    back_conv = lax.dot_general(
        grad_hidden.reshape(-1, channels),
        conv_full,
        (((1,), (1,)), ((), ())),
        preferred_element_type=jnp.float32,
    )
    grad_act = fold_taps(
        back_conv.reshape(tile_total, tile_side, tile_side, 9 * channels), tile_side, 1
    )
    grad_pre = grad_act * sigmoid_v * (1.0 + pre_act * (1.0 - sigmoid_v))
    scaled = grad_pre * norm_gain
    mean_one = group_mean(jnp.sum(scaled, axis=(1, 2)), member, per_group)[:, None, None, :]
    mean_two = group_mean(jnp.sum(scaled * normed, axis=(1, 2)), member, per_group)[
        :, None, None, :
    ]
    grad_input = (grad_resid + inv_std * (scaled - mean_one - normed * mean_two)).astype(
        jnp.bfloat16
    )
    affine = jnp.stack(
        [
            jnp.sum(grad_pre * normed, axis=(0, 1, 2)),
            jnp.sum(grad_pre, axis=(0, 1, 2)),
            jnp.sum(grad_resid, axis=(0, 1, 2)),
        ]
    )
    return (block_output, grad_input, activated, grad_hidden, affine)


def body(
    latents,
    bucket,
    cotangent,
    tile_count,
    cond_table,
    norm_gain,
    norm_shift,
    conv_bias,
    down_bias,
    conv_weight,
    down_weight,
):
    conv_full, down_full = (
        lax.all_gather(conv_weight, "fsdp", axis=0, tiled=True),
        lax.all_gather(down_weight, "fsdp", axis=0, tiled=True),
    )
    params = (cond_table, norm_gain, norm_shift, conv_bias, down_bias, conv_full, down_full)
    slot_total = latents.shape[0]
    tile_side = latents.shape[1]
    channels = latents.shape[3]
    half_side = tile_side // 2
    per_block = 2
    block_rows = per_block * tile_side * tile_side
    live_count = tile_count[0]
    slot_ids = jnp.arange(slot_total, dtype=jnp.int32)
    masked_cot = jnp.where(
        (slot_ids < live_count)[:, None, None, None], cotangent, jnp.zeros_like(cotangent)
    )
    buffer_slots = latents.shape[0]
    start_state = (
        jnp.zeros((buffer_slots, half_side, half_side, channels), jnp.bfloat16),
        jnp.zeros((buffer_slots, tile_side, tile_side, channels), jnp.bfloat16),
        jnp.zeros((buffer_slots, tile_side, tile_side, channels), jnp.bfloat16),
        jnp.zeros((buffer_slots, tile_side, tile_side, channels), jnp.bfloat16),
        jnp.zeros((3, channels), jnp.float32),
    )

    def block_step(block_index, carry_state):
        block_start = block_index * per_block
        results = tile_pass(
            lax.dynamic_slice_in_dim(latents, block_start, per_block, 0),
            lax.dynamic_slice_in_dim(bucket, block_start, per_block, 0),
            lax.dynamic_slice_in_dim(masked_cot, block_start, per_block, 0),
            params,
        )
        updated = tuple(
            (
                lax.dynamic_update_slice_in_dim(
                    carry_state[position], results[position], block_start, 0
                )
                for position in range(4)
            )
        )
        return updated + (carry_state[4] + results[4],)

    own_work = lax.fori_loop(0, slot_total // per_block, block_step, start_state)
    block_output, grad_input = (own_work[0], own_work[1])
    grad_pairs = [(own_work[2], own_work[3], 0, slot_total // per_block)]
    affine = own_work[4]
    block_output = jnp.where(
        (slot_ids < live_count)[:, None, None, None], block_output, jnp.zeros_like(block_output)
    )
    loss_scale = 4.0 / math.sqrt(
        tile_side * tile_side * slot_total * lax.axis_size("dp") * lax.axis_size("fsdp")
    )
    patch_pairs = [
        (tap_patches(act_buf), hid_buf.reshape(-1, channels), first_block, last_block)
        for act_buf, hid_buf, first_block, last_block in grad_pairs
    ]

    def row_term(patch_block, hid_block):
        return lax.dot_general(
            patch_block, hid_block, (((0,), (0,)), ((), ())), preferred_element_type=jnp.float32
        )

    term_sum = jnp.zeros(
        (9 * channels // lax.axis_size("fsdp") * lax.axis_size("fsdp"), channels), jnp.float32
    )
    patch_buf, hid_rows, first_block, last_block = patch_pairs[0]

    def add_block(block_index, running):
        row_first = block_index * block_rows
        patch_block = lax.dynamic_slice_in_dim(patch_buf, row_first, block_rows, 0)
        hid_block = lax.dynamic_slice_in_dim(hid_rows, row_first, block_rows, 0)
        return running + row_term(patch_block, hid_block)

    term_sum = lax.fori_loop(first_block, last_block, add_block, term_sum)
    row_part = lax.psum_scatter(term_sum * loss_scale, "fsdp", scatter_dimension=0, tiled=True)
    grad_conv = lax.psum(row_part, "dp")
    grad_affine = lax.psum(affine * loss_scale, ("dp", "fsdp"))
    return (block_output, grad_input, grad_conv, grad_affine)


def solution(mesh):
    placed = (
        P(("dp", "fsdp"), None, None, None),
        P(("dp", "fsdp")),
        P(("dp", "fsdp"), None, None, None),
        P(("dp", "fsdp")),
        P(),
        P(),
        P(),
        P(),
        P(),
        P("fsdp", None),
        P("fsdp", None),
    )
    return jax.shard_map(
        body,
        mesh=mesh,
        in_specs=placed,
        out_specs=(
            P(("dp", "fsdp"), None, None, None),
            P(("dp", "fsdp"), None, None, None),
            P("fsdp", None),
            P(),
        ),
        check_vma=False,
    )
```

profile of v0, /device:TPU:2, one launch (start us, length us, event | category | flops | bytes accessed | tf_op | source)
XLA Modules:
  0.0 608.4 jit_solution(4514434367798516532)
XLA Ops:
  10.4 75.9 %all-gather.3.cloned.1.call-done = bf16[5760,640]{1,0:T(8,128)(2,1)} async-done(((bf16[360,640]{1,0:T(8,128)(2,1)}), bf16[5760,640]{1,0:T(8,128)(2,1)}) %all-gather.3.cloned.1.call-update) | async-done | bytes 7372816 | tf_op jit(solution)/shard_map/all_gather | solution.py:140
  86.3 74.5 %all-gather.5.cloned.1.call-done = bf16[5760,640]{1,0:T(8,128)(2,1)} async-done(((bf16[360,640]{1,0:T(8,128)(2,1)}), bf16[5760,640]{1,0:T(8,128)(2,1)}) %all-gather.5.cloned.1.call-update) | async-done | bytes 7372816 | tf_op jit(solution)/shard_map/all_gather | solution.py:141
  160.9 125.5 %while.48 = (s32[]{:T(128)}, bf16[4,4,4,640]{3,2,1,0:T(4,128)(2,1)S(1)}, bf16[4,8,8,640]{3,2,1,0:T(8,128)(2,1)S(1)}, bf16[4,8,8,640]{3,2,1,0:T(8,128)(2,1)S(1)},...) while((s32[]{:T(128)}, ...), condition=%wide.region_18.19_spmd.clone, body=%wide.region_0.18_spmd.clone.sunk | while | flops 2368990720 | bytes 76295824 | solution.py:182
  161.0 1.4 and_reduce_fusion.2
  169.6 5.4 fusion.187
  175.3 1.4 scatter_fusion
  176.8 1.4 scatter_fusion.1
  178.2 1.4 scatter_fusion.2
  179.7 1.4 scatter_fusion.3
  181.1 1.4 scatter_fusion.4
  182.6 1.4 scatter_fusion.5
  184.0 1.4 scatter_fusion.6
  185.5 1.4 scatter_fusion.7
  186.9 1.4 scatter_fusion.8
  188.5 5.3 fusion.188
  193.9 1.4 slice_add_fusion.12
  195.5 1.7 scatter-add.242
  197.2 2.8 add_select_fusion.5
  200.0 1.5 scatter-add.243
  211.8 4.5 fusion.205
  219.2 4.4 fusion.206
  223.6 1.4 and_reduce_fusion.2
  232.3 5.4 fusion.187
  238.0 1.4 scatter_fusion
  239.5 1.4 scatter_fusion.1
  240.9 1.4 scatter_fusion.2
  242.4 1.4 scatter_fusion.3
  243.8 1.4 scatter_fusion.4
  245.2 1.4 scatter_fusion.5
  246.7 1.4 scatter_fusion.6
  248.1 1.4 scatter_fusion.7
  249.6 1.4 scatter_fusion.8
  251.2 5.3 fusion.188
  256.5 1.4 slice_add_fusion.12
  258.2 1.7 scatter-add.242
  259.9 2.8 add_select_fusion.5
  262.7 1.5 scatter-add.243
  274.4 4.5 fusion.205
  281.9 4.4 fusion.206
  287.2 1.6 copy-done.2
  288.8 21.7 %while.49 = (s32[]{:T(128)}, f32[5760,640]{1,0:T(8,128)}, bf16[256,5760]{1,0:T(8,128)(2,1)}, bf16[256,640]{1,0:T(8,128)(2,1)S(1)}, s32[]{:T(128)}, /*index=5*/s32[]{:T(128)}, s32[]{:T(128)}, s32[]{:T(128)}) while((s32[]{:T(128)}, f32[5760,640]{1,0:T(8,128)}, bf16[256,5760]{1,0:T(8,128)(2,1)}, bf16[256,640]{1,0:T(8,128)(2,1)S(1)}, ...), condition=%wide.region_20.21_spmd.clone, body=%wide.region_19.20_spmd.clone.sunk | while | flops 951091200 | bytes 31131284 | solution.py:213
  288.8 8.7 %select_add_fusion.2 = f32[5760,640]{1,0:T(8,128)} fusion(f32[5760,640]{1,0:T(8,128)} %get-tuple-element.1146, pred[]{:T(512)S(6)} %compare.279, bf16[256,5760]{1,0:T(8,128)(2,1)} %get-tuple-element.1155, s32[]{:T(128)S(6)} %select_n.77, bf16[256,640]{1,0:T(8,128)(2,1)S(1)} %get-tuple-element.1156), kind=kOutput, calls=%fused_computation.159.clone.1 | convolution fusion | flops 951091200 | bytes 31131136 | tf_op jit(solution)/shard_map/while/body/eval_jaxpr/dot_general | solution.py:198
  297.5 13.0 %select_add_fusion.2 = f32[5760,640]{1,0:T(8,128)} fusion(f32[5760,640]{1,0:T(8,128)} %get-tuple-element.1146, pred[]{:T(512)S(6)} %compare.279, bf16[256,5760]{1,0:T(8,128)(2,1)} %get-tuple-element.1155, s32[]{:T(128)S(6)} %select_n.77, bf16[256,640]{1,0:T(8,128)(2,1)S(1)} %get-tuple-element.1156), kind=kOutput, calls=%fused_computation.159.clone.1 | convolution fusion | flops 951091200 | bytes 31131136 | tf_op jit(solution)/shard_map/while/body/eval_jaxpr/dot_general | solution.py:198
  310.5 11.3 %broadcast_multiply_fusion = f32[5760,640]{1,0:T(8,128)} fusion(f32[5760,640]{1,0:T(8,128)} %get-tuple-element.736), kind=kLoop, calls=%fused_computation.163 | loop fusion | flops 3686400 | bytes 29491200 | tf_op jit(solution)/shard_map/mul | solution.py:214
  321.9 138.6 %reduce-scatter.4.cloned.1.call-done = f32[360,640]{1,0:T(8,128)} async-done(((f32[5760,640]{1,0:T(8,128)}), f32[360,640]{1,0:T(8,128)}) %reduce-scatter.4.cloned.1.call-update) | async-done | bytes 921616
  460.5 74.8 %psum.15 = f32[3,640]{1,0:T(4,128)} all-reduce(f32[3,640]{1,0:T(4,128)S(1)} %broadcast_multiply_fusion.1), channel_id=1, replica_groups=mesh['dp'=16,'fsdp'=16] {'dp','fsdp'}, use_global_device_ids=true, to_apply=%region_23.24 | all-reduce | flops 1920 | bytes 15360 | tf_op jit(solution)/shard_map/psum | solution.py:216
  536.0 63.7 %all-reduce.7.cloned.1.call-done = f32[360,640]{1,0:T(8,128)} async-done(((f32[360,640]{1,0:T(8,128)}), f32[360,640]{1,0:T(8,128)}) %all-reduce.7.cloned.1.call-update) | async-done | bytes 921616 | tf_op jit(solution)/shard_map/psum | solution.py:215
  599.7 2.2 copy.147
  (246 shorter events, 46.5 us)
Async XLA Ops:
  7.2 79.1 %all-gather.3.cloned.1.call-start = ((), (), s32[]{:S(2)}) async-start(), calls=%async_computation.1 | async-start | bytes 7833600 | tf_op jit(solution)/shard_map/all_gather | solution.py:140
  7.9 152.9 %all-gather.5.cloned.1.call-start = ((), (), s32[]{:S(2)}) async-start(), calls=%async_computation.2 | async-start | bytes 7833600 | tf_op jit(solution)/shard_map/all_gather | solution.py:141
  8.6 451.8 %reduce-scatter.4.cloned.1.call-start = ((), (), s32[]{:S(2)}) async-start(), calls=%async_computation.4 | async-start | bytes 15667200
  9.4 151.5 %copy-start.8 = (pred[4]{0:T(512)(128)(4,1)}, pred[4]{0:T(512)(128)(4,1)S(1)}, u32[]{:S(2)}) copy-start(pred[4]{0:T(512)(128)(4,1)S(1)} %iota_compare_fusion.9) | copy-start | bytes 16
  193.8 1.6 copy-start
  204.0 5.3 copy-start.1
  204.0 5.3 copy-start.3
  204.0 5.3 copy-start.4
  209.4 2.4 copy-start.7
  211.7 7.5 %copy-start.6 = (f32[640]{0:T(1024)S(1)}, f32[640]{0:T(1024)}, u32[]{:S(2)}) copy-start(f32[640]{0:T(1024)} %get-tuple-element.1127) | copy-start | bytes 7684 | tf_op jit(solution)/shard_map/while
  256.5 1.6 copy-start
  266.7 5.3 copy-start.1
  266.7 5.3 copy-start.3
  266.7 5.3 copy-start.4
  272.0 2.4 copy-start.7
  274.4 7.5 %copy-start.6 = (f32[640]{0:T(1024)S(1)}, f32[640]{0:T(1024)}, u32[]{:S(2)}) copy-start(f32[640]{0:T(1024)} %get-tuple-element.1127) | copy-start | bytes 7684 | tf_op jit(solution)/shard_map/while
  286.5 0.7 copy-start.5
  287.2 1.6 copy-start.2
  321.8 213.5 %copy-start.9 = (pred[4]{0:T(512)(128)(4,1)S(1)}, pred[4]{0:T(512)(128)(4,1)}, u32[]{:S(2)}) copy-start(pred[4]{0:T(512)(128)(4,1)} %copy-done.8) | copy-start | bytes 16
  321.8 277.9 %all-reduce.7.cloned.1.call-start = ((), (), s32[]{:S(2)}) async-start(), calls=%async_computation.3 | async-start | bytes 1843200 | tf_op jit(solution)/shard_map/psum | solution.py:215
Sparse Core Ops, SparseCore 0:
  10.8 75.4 all-gather.2
  89.1 71.6 all-gather.4
  321.9 138.4 reduce-scatter.3
  463.0 136.6 all-reduce.6
where the time goes:
time: 610 us; the launch traced here: 608 us
  waiting for transfers between devices  354 us (58%)
  blocking collectives  74.8 us (12%)
  matrix products  68.5 us (11%)
  other arithmetic  67.4 us (11%)
  local copies, waits for them, and re-layouts  27.4 us (4%)
  between operations  14.6 us (2%)
    unnamed x5, waiting for transfers between devices  140 us
    all_gather x1, waiting for transfers between devices, body(): lax.all_gather(conv_weight, 'fsdp', axis=0, tiled=True)  75.9 us
    psum x1, blocking collectives, body(): grad_affine = lax.psum(affine * loss_scale, ('dp', 'fsdp'))  74.8 us
    all_gather x1, waiting for transfers between devices, body(): lax.all_gather(down_weight, 'fsdp', axis=0, tiled=True)  74.5 us
    psum x1, waiting for transfers between devices, body(): grad_conv = lax.psum(row_part, 'dp')  63.7 us
    scatter-add x22, other arithmetic, fold_taps(): padded.at[:, row_off:stop_row:stride, col_off:stop_col:stride, :]  29.1 us
    dot_general x2, matrix products, row_term(): lax.dot_general(patch_block, hid_block, (((0,), (0,)), ((), ())), preferr...  21.7 us
  transfers between devices with their start and end apart: 4, of which 4 were waited for; matrix products, arithmetic and copies ran while one was open for 0% of the time, Pallas kernels for 0%

commit v1 on v0

v1 whole, which is shorter than its diff:
```python
import math

import jax
import jax.numpy as jnp
from jax import lax
from jax.sharding import PartitionSpec as P

GROUPS = 32
CONV_DIMS = ("NHWC", "HWIO", "NHWC")
BACK_DIMS = ("NHWC", "HWOI", "NHWC")


def group_mean(channel_sums, per_group):
    tiles, channels = channel_sums.shape
    width = channels // GROUPS
    grouped = channel_sums.reshape(tiles, GROUPS, width).sum(axis=-1) / per_group
    return jnp.repeat(grouped, width, axis=1)


def shifted(padded, tap, tile_side):
    row_off = tap // 3
    col_off = tap % 3
    return lax.dynamic_slice(
        padded,
        (0, row_off, col_off, 0),
        (padded.shape[0], tile_side, tile_side, padded.shape[3]),
    )


def body(
    latents,
    bucket,
    cotangent,
    tile_count,
    cond_table,
    norm_gain,
    norm_shift,
    conv_bias,
    down_bias,
    conv_weight,
    down_weight,
):
    slot_total, tile_side, _, channels = latents.shape
    row_block = conv_weight.shape[0]
    conv_full = lax.all_gather(conv_weight, "fsdp", axis=0, tiled=True)
    down_full = lax.all_gather(down_weight, "fsdp", axis=0, tiled=True)
    conv_kernel = conv_full.reshape(3, 3, channels, channels)
    down_kernel = down_full.reshape(3, 3, channels, channels)

    live = jnp.arange(slot_total, dtype=jnp.int32) < tile_count[0]
    live4 = live[:, None, None, None]
    masked_cot = jnp.where(live4, cotangent, jnp.zeros_like(cotangent))

    per_group = tile_side * tile_side * (channels // GROUPS)
    values = latents.astype(jnp.float32)
    center = group_mean(jnp.sum(values, axis=(1, 2)), per_group)
    deviation = values - center[:, None, None, :]
    spread = group_mean(jnp.sum(deviation * deviation, axis=(1, 2)), per_group)
    inv_std = lax.rsqrt(spread + 1e-05)[:, None, None, :]
    normed = deviation * inv_std
    pre_act = normed * norm_gain + norm_shift
    sigmoid_v = jax.nn.sigmoid(pre_act)
    activated = (pre_act * sigmoid_v).astype(jnp.bfloat16)
    act_all = lax.all_gather(activated, "fsdp", axis=0, tiled=True)

    conditioning = cond_table[bucket]
    conv_out = lax.conv_general_dilated(
        activated,
        conv_kernel,
        (1, 1),
        ((1, 1), (1, 1)),
        dimension_numbers=CONV_DIMS,
        preferred_element_type=jnp.float32,
    )
    conv_out = conv_out + conv_bias + conditioning[:, None, None, :]
    residual = (values + conv_out).astype(jnp.bfloat16)
    down_out = lax.conv_general_dilated(
        residual,
        down_kernel,
        (2, 2),
        ((1, 1), (1, 1)),
        dimension_numbers=CONV_DIMS,
        preferred_element_type=jnp.float32,
    )
    block_output = (down_out + down_bias).astype(jnp.bfloat16)
    block_output = jnp.where(live4, block_output, jnp.zeros_like(block_output))

    grad_resid = lax.conv_general_dilated(
        masked_cot,
        down_kernel[::-1, ::-1],
        (1, 1),
        ((1, 2), (1, 2)),
        lhs_dilation=(2, 2),
        dimension_numbers=BACK_DIMS,
        preferred_element_type=jnp.float32,
    )
    grad_hidden = grad_resid.astype(jnp.bfloat16)
    grad_act = lax.conv_general_dilated(
        grad_hidden,
        conv_kernel[::-1, ::-1],
        (1, 1),
        ((1, 1), (1, 1)),
        dimension_numbers=BACK_DIMS,
        preferred_element_type=jnp.float32,
    )
    grad_pre = grad_act * sigmoid_v * (1.0 + pre_act * (1.0 - sigmoid_v))
    scaled = grad_pre * norm_gain
    mean_one = group_mean(jnp.sum(scaled, axis=(1, 2)), per_group)[:, None, None, :]
    mean_two = group_mean(jnp.sum(scaled * normed, axis=(1, 2)), per_group)[:, None, None, :]
    grad_input = (grad_resid + inv_std * (scaled - mean_one - normed * mean_two)).astype(
        jnp.bfloat16
    )
    affine = jnp.stack(
        [
            jnp.sum(grad_pre * normed, axis=(0, 1, 2)),
            jnp.sum(grad_pre, axis=(0, 1, 2)),
            jnp.sum(grad_resid, axis=(0, 1, 2)),
        ]
    )
    affine_hi = affine.astype(jnp.bfloat16)
    affine_lo = (affine - affine_hi.astype(jnp.float32)).astype(jnp.bfloat16)
    hid_rows = grad_hidden.reshape(-1, channels)
    sent = jnp.concatenate([hid_rows, affine_hi, affine_lo], axis=0)
    sent_all = lax.all_gather(sent, "fsdp", axis=0, tiled=False)
    hid_all = sent_all[:, : hid_rows.shape[0]].reshape(-1, channels)
    affine_parts = sent_all[:, hid_rows.shape[0] :].astype(jnp.float32)
    affine_fsdp = jnp.sum(affine_parts[:, :3] + affine_parts[:, 3:], axis=0)

    first_row = lax.axis_index("fsdp") * row_block
    first_tap = first_row // channels
    first_chan = first_row % channels
    span = (row_block + channels - 1) // channels + 1
    act_pad = jnp.pad(act_all, ((0, 0), (1, 1), (1, 1), (0, 0)))
    taps = [
        shifted(act_pad, jnp.minimum(first_tap + extra, 8), tile_side) for extra in range(span)
    ]
    tap_cols = jnp.concatenate(taps, axis=-1)
    own_cols = lax.dynamic_slice_in_dim(tap_cols, first_chan, row_block, axis=3)
    weight_term = lax.dot_general(
        own_cols.reshape(-1, row_block),
        hid_all,
        (((0,), (0,)), ((), ())),
        preferred_element_type=jnp.float32,
    )
    loss_scale = 4.0 / math.sqrt(
        tile_side * tile_side * slot_total * lax.axis_size("dp") * lax.axis_size("fsdp")
    )
    summed = lax.psum(
        jnp.concatenate([weight_term, affine_fsdp], axis=0) * loss_scale, "dp"
    )
    grad_conv = summed[:row_block]
    grad_affine = summed[row_block:]
    return (block_output, grad_input, grad_conv, grad_affine)


def solution(mesh):
    placed = (
        P(("dp", "fsdp"), None, None, None),
        P(("dp", "fsdp")),
        P(("dp", "fsdp"), None, None, None),
        P(("dp", "fsdp")),
        P(),
        P(),
        P(),
        P(),
        P(),
        P("fsdp", None),
        P("fsdp", None),
    )
    return jax.shard_map(
        body,
        mesh=mesh,
        in_specs=placed,
        out_specs=(
            P(("dp", "fsdp"), None, None, None),
            P(("dp", "fsdp"), None, None, None),
            P("fsdp", None),
            P(),
        ),
        check_vma=False,
    )
```

time: 610 us -> 457 us (0.75)
  blocking collectives: 74.8 us -> 0 us
  other arithmetic: 67.4 us -> 12.5 us
  matrix products: 68.5 us -> 27.6 us
  waiting for transfers between devices: 354 us -> 381 us
  local copies, waits for them, and re-layouts: 27.4 us -> 20.6 us
    unnamed x5, waiting for transfers between devices: 140 us -> 1.43 us
    all_gather x2 -> x4, waiting for transfers between devices: 150 us -> 256 us  [the longest x1 73.6 us: body(): down_full = lax.all_gather(down_weight, 'fsdp', axis=0, tiled=True)]
    psum x1 -> x0, blocking collectives: 74.8 us -> none  [body(): grad_affine = lax.psum(affine * loss_scale, ('dp', 'fsdp'))]
    dot_general x28 -> x1, matrix products: 68.5 us -> 2.51 us  [body(): lax.dot_general(own_cols.reshape(-1, row_block), hid_all, (((0,), (0,)),...]
    psum x1, waiting for transfers between devices: 63.7 us -> 124 us  [body(): lax.psum(jnp.concatenate([weight_term, affine_fsdp], axis=0) * loss_scale...]
    scatter-add x22 -> x0, other arithmetic: 29.1 us -> none  [fold_taps(): padded.at[:, row_off:stop_row:stride, col_off:stop_col:stride, :]]
    conv_general_dilated x0 -> x3, matrix products: none -> 25.1 us  [the longest x1 12 us: body(): lax.conv_general_dilated(residual, down_kernel, (2, 2), ((1, 1), (1, 1)),...]
    add x12 -> x0, other arithmetic: 11.1 us -> none  [the longest x10 11.1 us: fold_taps(): padded.at[:, row_off:stop_row:stride, col_off:stop_col:stride, :]]
  transfers between devices with their start and end apart: 4 -> 5, of which waited for: 4 -> 5; matrix products, arithmetic and copies ran while one was open for 0% -> 9% of each run, Pallas kernels for 0% -> 0%
where the time goes in v1:
time: 457 us
  waiting for transfers between devices  381 us (83%)
  matrix products  27.6 us (6%)
  local copies, waits for them, and re-layouts  20.6 us (5%)
  between operations  14.8 us (3%)
  other arithmetic  12.5 us (3%)
    psum x1, waiting for transfers between devices, body(): lax.psum(jnp.concatenate([weight_term, affine_fsdp], axis=0) * loss_scale...  124 us
    all_gather x1, waiting for transfers between devices, body(): down_full = lax.all_gather(down_weight, 'fsdp', axis=0, tiled=True)  73.6 us
    all_gather x1, waiting for transfers between devices, body(): conv_full = lax.all_gather(conv_weight, 'fsdp', axis=0, tiled=True)  69 us
    all_gather x1, waiting for transfers between devices, body(): act_all = lax.all_gather(activated, 'fsdp', axis=0, tiled=True)  62 us
    all_gather x1, waiting for transfers between devices, body(): sent_all = lax.all_gather(sent, 'fsdp', axis=0, tiled=False)  51.1 us
    conv_general_dilated x1, matrix products, body(): lax.conv_general_dilated(residual, down_kernel, (2, 2), ((1, 1), (1, 1)),...  12 us
    dynamic_slice x1, local copies, waits for them, and re-layouts, shifted(): lax.dynamic_slice(padded, (0, row_off, col_off, 0), (padded.shape[0], til...  11.6 us
  transfers between devices with their start and end apart: 5, of which 5 were waited for; matrix products, arithmetic and copies ran while one was open for 9% of the time, Pallas kernels for 0%

profile of v1, /device:TPU:2, one launch (start us, length us, event | category | flops | bytes accessed | tf_op | source)
XLA Modules:
  0.0 456.9 jit_solution(273286597701240359)
XLA Ops:
  7.2 0.0 all-gather.9.cloned.1.call-start
  7.3 0.7 all-gather.9.cloned.1.call-update
  7.9 0.0 all-gather.7.cloned.1.call-start
  8.0 0.7 all-gather.7.cloned.1.call-update
  8.7 0.0 all-gather.11.cloned.1.call-start
  9.4 1.2 convert_reduce_fusion
  10.6 0.1 reshape.57
  10.7 0.1 reduce_sum.109
  10.8 0.1 broadcast_in_dim.35
  10.9 0.1 sub.39
  11.0 1.3 fusion.20
  12.3 0.1 reshape.58
  12.4 0.1 reduce_sum.111
  12.5 0.1 broadcast_in_dim.36
  12.6 0.1 rsqrt.12
  12.8 73.6 %all-gather.9.cloned.1.call-done = bf16[5760,640]{1,0:T(8,128)(2,1)} async-done(((bf16[360,640]{1,0:T(8,128)(2,1)}), bf16[5760,640]{1,0:T(8,128)(2,1)}) %all-gather.9.cloned.1.call-update) | async-done | bytes 7372816 | tf_op jit(solution)/shard_map/all_gather | solution.py:46
  86.4 5.5 %fusion.28 = (bf16[4,8,8,640]{3,0,2,1:T(4,128)(2,1)S(1)}, f32[4,8,8,640]{3,0,2,1:T(4,128)S(1)}) fusion(bf16[3,3,640,640]{3,2,1,0:T(8,128)(2,1)} %bitcast.23, bf16[4,4,4,640]{3,2,1,0:T(4,128)(2,1)} %param.13, pred[4]{0:T(512)(128)(4,1)S(1)} %iota_compare_fusion), kind=kOutput, calls=%fused_computation.55 | convolution fusion | flops 396697600 | bytes 8437764 | tf_op jit(solution)/shard_map/conv_general_dilated | solution.py:88
  91.8 69.0 %all-gather.7.cloned.1.call-done = bf16[5760,640]{1,0:T(8,128)(2,1)} async-done(((bf16[360,640]{1,0:T(8,128)(2,1)}), bf16[5760,640]{1,0:T(8,128)(2,1)}) %all-gather.7.cloned.1.call-update) | async-done | bytes 7372816 | tf_op jit(solution)/shard_map/all_gather | solution.py:45
  160.8 7.6 %fusion.19 = (f32[640]{0:T(1024)S(1)}, f32[4,640]{1,0:T(4,128)S(1)}, f32[4,640]{1,0:T(4,128)S(1)}, f32[640]{0:T(1024)S(1)}, f32[4,8,8,640]{3,0,2,1:T(4,128)S(1)}) fusion(f32[4,640]{1,0:T(4,128)S(1)} %rsqrt.12, f32[4,640]{1,0:T(4,128)S(1)} %sub.39, bf16[4,8,8,640]{3,2,1,0:T(8,128)(2,1)S(1)} %copy-done.1, f32[640]{0:T(1024)S(1)} %copy-done.4, ...), kind=kOutput, calls=%fused_computation.30 | convolution fusion | flops 1589241600 | bytes 8734720 | tf_op jit(solution)/shard_map/conv_general_dilated | solution.py:98
  168.4 0.1 reshape.62
  168.6 0.1 reduce_sum.115
  168.7 0.1 broadcast_in_dim.39
  168.7 0.1 mul.79
  168.9 0.1 reshape.61
  169.0 0.1 reduce_sum.113
  169.1 0.1 broadcast_in_dim.38
  169.2 0.1 sub.43
  169.3 1.6 fusion.27
  170.9 0.8 copy.27
  171.7 0.0 all-gather.13.cloned.1.call-start
  171.9 0.8 maximum_bitcast_fusion
  172.7 0.2 all-reduce.3.cloned.1.call-start
  173.1 0.6 gather_fusion
  173.7 62.0 %all-gather.11.cloned.1.call-done = bf16[64,8,8,640]{3,2,1,0:T(8,128)(2,1)} async-done(((bf16[4,8,8,640]{3,2,1,0:T(8,128)(2,1)}), bf16[64,8,8,640]{3,2,1,0:T(8,128)(2,1)}) %all-gather.11.cloned.1.call-update) | async-done | bytes 5242896 | tf_op jit(solution)/shard_map/all_gather | solution.py:64
  235.7 11.6 %pad_dynamic-slice_fusion = (bf16[64,8,8,640]{3,2,1,0:T(8,128)(2,1)}, bf16[64,8,8,640]{3,2,1,0:T(8,128)(2,1)}) fusion(s32[]{:T(128)S(6)} %select_n.59, s32[]{:T(128)S(6)} %select_n.61, bf16[64,8,8,640]{3,2,1,0:T(8,128)(2,1)} %all-gather.11.cloned.1.call-done, s32[]{:T(128)S(6)} %select_n.55, s32[]{:T(128)S(6)} %select_n.57), kind=kLoop, calls=%fused_computation.1 | loop fusion | bytes 15728656 | tf_op jit(solution)/shard_map/dynamic_slice | solution.py:23
  247.3 5.0 %fusion = bf16[64,8,8,360]{3,2,1,0:T(8,128)(2,1)S(1)} fusion(s32[]{:T(128)S(6)} %select_n.63, bf16[64,8,8,640]{3,2,1,0:T(8,128)(2,1)} %get-tuple-element.21, bf16[64,8,8,640]{3,2,1,0:T(8,128)(2,1)} %get-tuple-element.20), kind=kLoop, calls=%fused_computation.5 | loop fusion | flops 5898240 | bytes 13434884 | tf_op jit(solution)/shard_map/concatenate | solution.py:137
  252.3 51.1 %all-gather.13.cloned.1.call-done = bf16[16,262,640]{2,1,0:T(8,128)(2,1)} async-done(((bf16[1,262,640]{2,1,0:T(8,128)(2,1)}), bf16[16,262,640]{2,1,0:T(8,128)(2,1)}) %all-gather.13.cloned.1.call-update) | async-done | bytes 5365776 | tf_op jit(solution)/shard_map/all_gather | solution.py:124
  303.4 1.1 slice_convert_fusion
  304.4 0.1 fusion.21
  304.5 1.4 slice-done
  305.9 2.5 fusion.29
  308.4 1.0 maximum_multiply_fusion
  309.5 12.0 %fusion.6 = bf16[4,4,4,640]{3,0,2,1:T(4,128)(2,1)S(1)} fusion(bf16[3,3,640,640]{3,2,1,0:T(8,128)(2,1)} %bitcast.24, f32[640]{0:T(1024)S(1)} %copy-done.5, pred[4]{0:T(512)(128)(4,1)S(1)} %iota_compare_fusion, bf16[3,3,640,640]{3,2,1,0:T(8,128)(2,1)} %bitcast.27, f32[4,640]{1,0:T(4,128)S(1)} %gather_fusion, f32[640]{0:T(1024)S(1)} %copy-done.6, ...), kind=kOutput, calls=%fused_computation.14 | convolution fusion | flops 1985044480 | bytes 15196164 | tf_op jit(solution)/shard_map/conv_general_dilated | solution.py:77
  321.6 0.7 copy.29
  322.2 0.8 copy.30
  323.0 123.9 %all-reduce.3.cloned.1.call-done = f32[363,640]{1,0:T(8,128)} async-done(((f32[363,640]{1,0:T(8,128)}), f32[363,640]{1,0:T(8,128)}) %all-reduce.3.cloned.1.call-update) | async-done | bytes 929296 | tf_op jit(solution)/shard_map/psum | solution.py:148
  446.8 1.3 slice.31
  448.2 2.2 slice.30
  (33 shorter events, 0.2 us)
Async XLA Ops:
  7.2 165.9 %copy-start = (f32[40,640]{1,0:T(8,128)S(1)}, f32[40,640]{1,0:T(8,128)}, u32[]{:S(2)}) copy-start(f32[40,640]{1,0:T(8,128)} %param.15) | copy-start | bytes 307204
  7.2 153.7 %copy-start.1 = (bf16[4,8,8,640]{3,2,1,0:T(8,128)(2,1)S(1)}, bf16[4,8,8,640]{3,2,1,0:T(8,128)(2,1)}, u32[]{:S(2)}) copy-start(bf16[4,8,8,640]{3,2,1,0:T(8,128)(2,1)} %param.11) | copy-start | bytes 983044
  7.2 153.6 %copy-start.3 = (f32[640]{0:T(1024)S(1)}, f32[640]{0:T(1024)}, u32[]{:S(2)}) copy-start(f32[640]{0:T(1024)} %param.17) | copy-start | bytes 7684
  7.2 153.6 %copy-start.4 = (f32[640]{0:T(1024)S(1)}, f32[640]{0:T(1024)}, u32[]{:S(2)}) copy-start(f32[640]{0:T(1024)} %param.16) | copy-start | bytes 7684
  7.2 79.1 %all-gather.9.cloned.1.call-start = ((), (), s32[]{:S(2)}) async-start(), calls=%async_computation.1 | async-start | bytes 7833600 | tf_op jit(solution)/shard_map/all_gather | solution.py:46
  7.9 152.9 %all-gather.7.cloned.1.call-start = ((), (), s32[]{:S(2)}) async-start(), calls=%async_computation | async-start | bytes 7833600 | tf_op jit(solution)/shard_map/all_gather | solution.py:45
  8.7 227.0 %all-gather.11.cloned.1.call-start = ((), (), s32[]{:S(2)}) async-start(), calls=%async_computation.2 | async-start | bytes 5570560 | tf_op jit(solution)/shard_map/all_gather | solution.py:64
  160.8 12.2 %copy-start.7 = (s32[4]{0:T(128)S(1)}, s32[4]{0:T(128)}, u32[]{:S(2)}) copy-start(s32[4]{0:T(128)} %param.12) | copy-start | bytes 52
  171.7 131.6 %all-gather.13.cloned.1.call-start = ((), (), s32[]{:S(2)}) async-start(), calls=%async_computation.4 | async-start | bytes 5744640 | tf_op jit(solution)/shard_map/all_gather | solution.py:124
  172.7 274.1 %all-reduce.3.cloned.1.call-start = ((), (), s32[]{:S(2)}) async-start(), calls=%async_computation.3 | async-start | bytes 1884160 | tf_op jit(solution)/shard_map/psum | solution.py:148
  303.3 2.6 slice-start
  305.9 3.6 copy-start.5
  305.9 3.6 copy-start.6
  309.5 12.7 %copy-start.2 = (bf16[4,8,8,640]{3,0,2,1:T(4,128)(2,1)S(1)}, bf16[4,8,8,640]{3,0,2,1:T(4,128)(2,1)}, u32[]{:S(2)}) copy-start(bf16[4,8,8,640]{3,0,2,1:T(4,128)(2,1)} %get-tuple-element.23) | copy-start | bytes 983044
Sparse Core Ops, SparseCore 0:
  10.8 75.4 all-gather.8
  89.2 71.6 all-gather.6
  171.9 63.7 all-gather.10
  238.9 64.4 all-gather.12
  309.6 137.2 all-reduce.2

commit v2 on v1

--- a/solution.py
+++ b/solution.py
@@ -25,6 +25,31 @@
         (0, row_off, col_off, 0),
         (padded.shape[0], tile_side, tile_side, padded.shape[3]),
     )
+
+
+def halving_doubling_sum(block, axis):
+    size = lax.axis_size(axis)
+    levels = size.bit_length() - 1
+    if size != 1 << levels or levels == 0:
+        return lax.psum(block, axis)
+    order = [0, levels - 1] + list(range(1, levels - 1)) if levels > 1 else [0]
+    rows = block.shape[0]
+    padded_rows = -(-rows // size) * size
+    cur = jnp.pad(block, ((0, padded_rows - rows), (0, 0)))
+    index = lax.axis_index(axis)
+    for level in order:
+        half = cur.shape[0] // 2
+        low = ((index >> level) & 1) == 0
+        send = jnp.where(low, cur[half:], cur[:half])
+        keep = jnp.where(low, cur[:half], cur[half:])
+        pairs = [(i, i ^ (1 << level)) for i in range(size)]
+        cur = keep + lax.ppermute(send, axis, pairs)
+    for level in reversed(order):
+        low = ((index >> level) & 1) == 0
+        pairs = [(i, i ^ (1 << level)) for i in range(size)]
+        other = lax.ppermute(cur, axis, pairs)
+        cur = jnp.where(low, jnp.concatenate([cur, other]), jnp.concatenate([other, cur]))
+    return cur[:rows]
 
 
 def body(
@@ -85,14 +110,19 @@
     block_output = (down_out + down_bias).astype(jnp.bfloat16)
     block_output = jnp.where(live4, block_output, jnp.zeros_like(block_output))
 
-    grad_resid = lax.conv_general_dilated(
-        masked_cot,
+    cot_all = lax.all_gather(masked_cot, "fsdp", axis=0, tiled=True)
+    resid_all = lax.conv_general_dilated(
+        cot_all,
         down_kernel[::-1, ::-1],
         (1, 1),
         ((1, 2), (1, 2)),
         lhs_dilation=(2, 2),
         dimension_numbers=BACK_DIMS,
         preferred_element_type=jnp.float32,
+    )
+    hid_all = resid_all.astype(jnp.bfloat16).reshape(-1, channels)
+    grad_resid = lax.dynamic_slice_in_dim(
+        resid_all, lax.axis_index("fsdp") * slot_total, slot_total, axis=0
     )
     grad_hidden = grad_resid.astype(jnp.bfloat16)
     grad_act = lax.conv_general_dilated(
@@ -117,14 +147,7 @@
             jnp.sum(grad_resid, axis=(0, 1, 2)),
         ]
     )
-    affine_hi = affine.astype(jnp.bfloat16)
-    affine_lo = (affine - affine_hi.astype(jnp.float32)).astype(jnp.bfloat16)
-    hid_rows = grad_hidden.reshape(-1, channels)
-    sent = jnp.concatenate([hid_rows, affine_hi, affine_lo], axis=0)
-    sent_all = lax.all_gather(sent, "fsdp", axis=0, tiled=False)
-    hid_all = sent_all[:, : hid_rows.shape[0]].reshape(-1, channels)
-    affine_parts = sent_all[:, hid_rows.shape[0] :].astype(jnp.float32)
-    affine_fsdp = jnp.sum(affine_parts[:, :3] + affine_parts[:, 3:], axis=0)
+    affine_fsdp = lax.psum(affine, "fsdp")
 
     first_row = lax.axis_index("fsdp") * row_block
     first_tap = first_row // channels
@@ -145,11 +168,10 @@
     loss_scale = 4.0 / math.sqrt(
         tile_side * tile_side * slot_total * lax.axis_size("dp") * lax.axis_size("fsdp")
     )
-    summed = lax.psum(
-        jnp.concatenate([weight_term, affine_fsdp], axis=0) * loss_scale, "dp"
-    )
+    stacked = jnp.concatenate([weight_term, affine_fsdp], axis=0) * loss_scale
+    summed = halving_doubling_sum(stacked, "dp")
     grad_conv = summed[:row_block]
-    grad_affine = summed[row_block:]
+    grad_affine = summed[row_block : row_block + affine.shape[0]]
     return (block_output, grad_input, grad_conv, grad_affine)
 
 

time: 457 us -> 399 us (0.87)
  waiting for transfers between devices: 381 us -> 228 us
  blocking collectives: 0 us -> 59.6 us
  starting transfers between devices: 0.38 us -> 19.2 us
  matrix products: 27.6 us -> 44.8 us
  other arithmetic: 12.5 us -> 6.79 us
    psum x1 -> x0, waiting for transfers between devices: 124 us -> none  [body(): lax.psum(jnp.concatenate([weight_term, affine_fsdp], axis=0) * loss_scale...]
    psum x0 -> x1, blocking collectives: none -> 59.6 us  [body(): affine_fsdp = lax.psum(affine, 'fsdp')]
    all_gather x1, waiting for transfers between devices: 62 us -> 4.54 us  [body(): act_all = lax.all_gather(activated, 'fsdp', axis=0, tiled=True)]
    ppermute x0 -> x8, waiting for transfers between devices: none -> 38.5 us  [the longest x4 25.1 us: halving_doubling_sum(): cur = keep + lax.ppermute(send, axis, pairs)]
    ppermute x0 -> x8, starting transfers between devices: none -> 19 us  [the longest x4 10.8 us: halving_doubling_sum(): cur = keep + lax.ppermute(send, axis, pairs)]
    conv_general_dilated x1, matrix products: 5.46 us -> 15.3 us  [body(): lax.conv_general_dilated(cot_all, down_kernel[::-1, ::-1], (1, 1), ((1, 2...]
    all_gather x1, waiting for transfers between devices: 69 us -> 59.1 us  [body(): conv_full = lax.all_gather(conv_weight, 'fsdp', axis=0, tiled=True)]
    all_gather x0 -> x1, local copies, waits for them, and re-layouts: none -> 7.88 us  [body(): act_all = lax.all_gather(activated, 'fsdp', axis=0, tiled=True)]
  transfers between devices with their start and end apart: 5 -> 12, of which waited for: 5 -> 11; matrix products, arithmetic and copies ran while one was open for 9% -> 8% of each run, Pallas kernels for 0% -> 0%
where the time goes in v2:
time: 399 us; the launch traced here: 397 us
  waiting for transfers between devices  228 us (57%)
  blocking collectives  59.6 us (15%)
  matrix products  44.8 us (11%)
  local copies, waits for them, and re-layouts  23.8 us (6%)
  starting transfers between devices  19.2 us (5%)
  between operations  14.9 us (4%)
  other arithmetic  6.79 us (2%)
    all_gather x1, waiting for transfers between devices, body(): down_full = lax.all_gather(down_weight, 'fsdp', axis=0, tiled=True)  74.5 us
    psum x1, blocking collectives, body(): affine_fsdp = lax.psum(affine, 'fsdp')  59.6 us
    all_gather x1, waiting for transfers between devices, body(): conv_full = lax.all_gather(conv_weight, 'fsdp', axis=0, tiled=True)  59.1 us
    all_gather x1, waiting for transfers between devices, body(): cot_all = lax.all_gather(masked_cot, 'fsdp', axis=0, tiled=True)  50.2 us
    ppermute x4, waiting for transfers between devices, halving_doubling_sum(): cur = keep + lax.ppermute(send, axis, pairs)  25.1 us
    conv_general_dilated x1, matrix products, body(): lax.conv_general_dilated(cot_all, down_kernel[::-1, ::-1], (1, 1), ((1, 2...  15.3 us
    ppermute x4, waiting for transfers between devices, halving_doubling_sum(): other = lax.ppermute(cur, axis, pairs)  13.3 us
    conv_general_dilated x1, matrix products, body(): lax.conv_general_dilated(residual, down_kernel, (2, 2), ((1, 1), (1, 1)),...  11.9 us
  transfers between devices with their start and end apart: 12, of which 11 were waited for; matrix products, arithmetic and copies ran while one was open for 8% of the time, Pallas kernels for 0%

profile of v2, /device:TPU:2, one launch (start us, length us, event | category | flops | bytes accessed | tf_op | source)
XLA Modules:
  0.0 397.2 jit_solution(12836842695800103598)
XLA Ops:
  7.9 1.0 copy_select_fusion
  8.9 0.7 copy.25
  9.6 0.7 all-gather.7.cloned.1.call-update
  10.4 0.7 all-gather.5.cloned.1.call-update
  11.1 1.2 convert_reduce_fusion
  12.4 0.1 reshape.50
  12.7 0.1 sub.36
  12.8 1.3 fusion.30
  14.1 0.1 reshape.51
  14.4 0.1 rsqrt.12
  14.5 50.2 %all-gather.9.cloned.1.call-done = bf16[64,4,4,640]{3,2,1,0:T(4,128)(2,1)} async-done(((bf16[4,4,4,640]{3,2,1,0:T(4,128)(2,1)}), bf16[64,4,4,640]{3,2,1,0:T(4,128)(2,1)}) %all-gather.9.cloned.1.call-update) | async-done | bytes 1310736 | tf_op jit(solution)/shard_map/all_gather | solution.py:113
  64.7 74.5 %all-gather.7.cloned.1.call-done = bf16[5760,640]{1,0:T(8,128)(2,1)} async-done(((bf16[360,640]{1,0:T(8,128)(2,1)}), bf16[5760,640]{1,0:T(8,128)(2,1)}) %all-gather.7.cloned.1.call-update) | async-done | bytes 7372816 | tf_op jit(solution)/shard_map/all_gather | solution.py:71
  139.2 15.3 %fusion.9 = f32[64,8,8,640]{3,0,2,1:T(8,128)} fusion(bf16[3,3,640,640]{3,2,1,0:T(8,128)(2,1)} %bitcast.17, bf16[64,4,4,640]{3,2,1,0:T(4,128)(2,1)} %all-gather.9.cloned.1.call-done), kind=kOutput, calls=%fused_computation.9 | convolution fusion | flops 6343884800 | bytes 19169280 | tf_op jit(solution)/shard_map/conv_general_dilated | solution.py:114
  154.5 59.1 %all-gather.5.cloned.1.call-done = bf16[5760,640]{1,0:T(8,128)(2,1)} async-done(((bf16[360,640]{1,0:T(8,128)(2,1)}), bf16[5760,640]{1,0:T(8,128)(2,1)}) %all-gather.5.cloned.1.call-update) | async-done | bytes 7372816 | tf_op jit(solution)/shard_map/all_gather | solution.py:70
  213.7 8.1 %fusion.29 = (f32[640]{0:T(1024)S(1)}, f32[4,640]{1,0:T(4,128)S(1)}, f32[4,640]{1,0:T(4,128)S(1)}, f32[640]{0:T(1024)S(1)}, f32[4,8,8,640]{3,0,2,1:T(4,128)S(1)}) fusion(f32[4,640]{1,0:T(4,128)S(1)} %rsqrt.12, f32[4,640]{1,0:T(4,128)S(1)} %sub.36, bf16[4,8,8,640]{3,2,1,0:T(8,128)(2,1)S(1)} %copy-done.1, f32[640]{0:T(1024)S(1)} %copy-done.3, ...), kind=kOutput, calls=%fused_computation.37 | convolution fusion | flops 1589241600 | bytes 8734724 | tf_op jit(solution)/shard_map/conv_general_dilated | solution.py:128
  221.7 0.1 reshape.55
  222.0 0.1 mul.83
  222.2 0.1 reshape.54
  222.5 0.1 sub.40
  222.6 2.4 dynamic-slice_reduce_fusion
  225.0 0.8 copy.27
  225.9 59.6 %psum.7 = f32[3,640]{1,0:T(4,128)S(1)} all-reduce(f32[3,640]{1,0:T(4,128)S(1)} %pad_maximum_fusion), channel_id=1, replica_groups=mesh['dp'=16,'fsdp'=16] {'fsdp'}, use_global_device_ids=true, to_apply=%region_11.12 | all-reduce | flops 1920 | bytes 15360 | tf_op jit(solution)/shard_map/psum | solution.py:150
  285.5 4.5 %all-gather.11.cloned.1.call-done = bf16[64,8,8,640]{3,2,1,0:T(8,128)(2,1)} async-done(((bf16[4,8,8,640]{3,2,1,0:T(8,128)(2,1)}), bf16[64,8,8,640]{3,2,1,0:T(8,128)(2,1)}) %all-gather.11.cloned.1.call-update) | async-done | bytes 5242896 | tf_op jit(solution)/shard_map/all_gather | solution.py:89
  290.0 7.9 %copy.28 = bf16[64,8,8,640]{3,0,2,1:T(8,128)(2,1)} copy(bf16[64,8,8,640]{3,2,1,0:T(8,128)(2,1)} %all-gather.11.cloned.1.call-done) | data formatting | bytes 10485760 | tf_op jit(solution)/shard_map/all_gather | solution.py:89
  297.9 9.6 %pad_dynamic-slice_fusion.2 = (bf16[64,8,8,640]{3,0,2,1:T(8,128)(2,1)}, bf16[64,8,8,640]{3,0,2,1:T(8,128)(2,1)}) fusion(s32[]{:T(128)S(6)} %select_n.145, s32[]{:T(128)S(6)} %select_n.147, bf16[64,8,8,640]{3,0,2,1:T(8,128)(2,1)} %copy.28, s32[]{:T(128)S(6)} %select_n.141, s32[]{:T(128)S(6)} %select_n.143), kind=kLoop, calls=%fused_computation.3 | loop fusion | bytes 15728656 | tf_op jit(solution)/shard_map/dynamic_slice | solution.py:23
  307.5 9.5 %fusion.4 = f32[360,640]{1,0:T(8,128)S(1)} fusion(f32[64,8,8,640]{3,0,2,1:T(8,128)} %fusion.9, s32[]{:T(128)S(6)} %select_n.149, bf16[64,8,8,640]{3,0,2,1:T(8,128)(2,1)} %get-tuple-element.23, bf16[64,8,8,640]{3,0,2,1:T(8,128)(2,1)} %get-tuple-element.22), kind=kOutput, calls=%fused_computation.8 | convolution fusion | flops 1895956480 | bytes 21893124 | tf_op jit(solution)/shard_map/dot_general | solution.py:162
  317.2 1.6 collective-permute-start
  318.8 11.4 %collective-permute-done = f32[184,640]{1,0:T(8,128)S(1)} collective-permute-done((f32[184,640]{1,0:T(8,128)S(1)}, f32[184,640]{1,0:T(8,128)S(1)}, u32[]{:S(2)}, u32[]{:S(2)}) %collective-permute-start) | collective-permute-done | bytes 471072 | tf_op jit(solution)/shard_map/ppermute | solution.py:46
  330.2 0.1 select_add_fusion
  330.3 0.7 collective-permute-start.1
  331.0 6.7 %collective-permute-done.1 = f32[92,640]{1,0:T(8,128)S(1)} collective-permute-done((f32[92,640]{1,0:T(8,128)S(1)}, f32[92,640]{1,0:T(8,128)S(1)}, u32[]{:S(2)}, u32[]{:S(2)}) %collective-permute-start.1) | collective-permute-done | bytes 235552 | tf_op jit(solution)/shard_map/ppermute | solution.py:46
  337.8 2.6 collective-permute-start.2
  340.4 4.8 %collective-permute-done.2 = f32[46,640]{1,0:T(8,128)S(1)} collective-permute-done((f32[46,640]{1,0:T(8,128)S(1)}, f32[46,640]{1,0:T(8,128)S(1)}, u32[]{:S(2)}, u32[]{:S(2)}) %collective-permute-start.2) | collective-permute-done | bytes 117792 | tf_op jit(solution)/shard_map/ppermute | solution.py:46
  345.2 5.9 %collective-permute-start.3 = (f32[23,640]{1,0:T(8,128)S(1)}, f32[23,640]{1,0:T(8,128)S(1)}, u32[]{:S(2)}, u32[]{:S(2)}) collective-permute-start(f32[23,640]{1,0:T(8,128)S(1)} %slice_select_fusion.3), channel_id=1, source_target_pairs={{0,64},{16,80},{32,96},{48,112},{64,0},{80,16},{96,32},{112,48},{1... | collective-permute-start | bytes 176648 | tf_op jit(solution)/shard_map/ppermute | solution.py:46
  351.1 2.3 collective-permute-done.3
  353.4 6.1 %collective-permute-start.4 = (f32[23,640]{1,0:T(8,128)S(1)}, f32[23,640]{1,0:T(8,128)S(1)}, u32[]{:S(2)}, u32[]{:S(2)}) collective-permute-start(f32[23,640]{1,0:T(8,128)S(1)} %select_add_fusion.3), channel_id=1, source_target_pairs={{0,64},{16,80},{32,96},{48,112},{64,0},{80,16},{96,32},{112,48},{1... | collective-permute-start | bytes 176648 | tf_op jit(solution)/shard_map/ppermute | solution.py:50
  359.6 2.4 collective-permute-done.4
  362.0 1.3 collective-permute-start.5
  363.3 5.9 %collective-permute-done.5 = f32[46,640]{1,0:T(8,128)S(1)} collective-permute-done((f32[46,640]{1,0:T(8,128)S(1)}, f32[46,640]{1,0:T(8,128)S(1)}, u32[]{:S(2)}, u32[]{:S(2)}) %collective-permute-start.5) | collective-permute-done | bytes 117792 | tf_op jit(solution)/shard_map/ppermute | solution.py:50
  369.2 0.7 collective-permute-start.6
  369.9 0.6 gather_fusion
  370.5 5.0 %collective-permute-done.6 = f32[92,640]{1,0:T(8,128)S(1)} collective-permute-done((f32[92,640]{1,0:T(8,128)S(1)}, f32[92,640]{1,0:T(8,128)S(1)}, u32[]{:S(2)}, u32[]{:S(2)}) %collective-permute-start.6) | collective-permute-done | bytes 235552 | tf_op jit(solution)/shard_map/ppermute | solution.py:50
  375.6 0.1 collective-permute-start.7
  375.7 11.9 %fusion.16 = bf16[4,4,4,640]{3,0,2,1:T(4,128)(2,1)S(1)} fusion(bf16[3,3,640,640]{3,2,1,0:T(8,128)(2,1)} %bitcast.18, f32[640]{0:T(1024)S(1)} %copy-done.4, pred[4]{0:T(512)(128)(4,1)S(1)} %iota_compare_fusion, bf16[3,3,640,640]{3,2,1,0:T(8,128)(2,1)} %bitcast.20, f32[4,640]{1,0:T(4,128)S(1)} %gather_fusion, f32[640]{0:T(1024)S(1)} %copy-done.5, ...), kind=kOutput, calls=%fused_computation.19 | convolution fusion | flops 1985044480 | bytes 15196164 | tf_op jit(solution)/shard_map/conv_general_dilated | solution.py:102
  387.5 0.7 copy.29
  388.2 0.8 copy.30
  389.1 1.0 slice.61
  390.0 0.6 slice.62
  (52 shorter events, 1.4 us)
Async XLA Ops:
  7.2 362.7 %copy-start = (f32[40,640]{1,0:T(8,128)S(1)}, f32[40,640]{1,0:T(8,128)}, u32[]{:S(2)}) copy-start(f32[40,640]{1,0:T(8,128)} %param.15) | copy-start | bytes 307204
  7.2 57.5 %all-gather.9.cloned.1.call-start = ((), (), s32[]{:S(2)}) async-start(), calls=%async_computation.2 | async-start | bytes 1392640 | tf_op jit(solution)/shard_map/all_gather | solution.py:113
  9.6 129.6 %all-gather.7.cloned.1.call-start = ((), (), s32[]{:S(2)}) async-start(), calls=%async_computation.1 | async-start | bytes 7833600 | tf_op jit(solution)/shard_map/all_gather | solution.py:71
  10.3 203.3 %all-gather.5.cloned.1.call-start = ((), (), s32[]{:S(2)}) async-start(), calls=%async_computation | async-start | bytes 7833600 | tf_op jit(solution)/shard_map/all_gather | solution.py:70
  11.1 278.9 %all-gather.11.cloned.1.call-start = ((), (), s32[]{:S(2)}) async-start(), calls=%async_computation.3 | async-start | bytes 5570560 | tf_op jit(solution)/shard_map/all_gather | solution.py:89
  139.2 74.5 %copy-start.1 = (bf16[4,8,8,640]{3,2,1,0:T(8,128)(2,1)S(1)}, bf16[4,8,8,640]{3,2,1,0:T(8,128)(2,1)}, u32[]{:S(2)}) copy-start(bf16[4,8,8,640]{3,2,1,0:T(8,128)(2,1)} %param.11) | copy-start | bytes 983044
  139.2 74.5 %copy-start.2 = (f32[640]{0:T(1024)S(1)}, f32[640]{0:T(1024)}, u32[]{:S(2)}) copy-start(f32[640]{0:T(1024)} %param.17) | copy-start | bytes 7684
  139.2 74.5 %copy-start.3 = (f32[640]{0:T(1024)S(1)}, f32[640]{0:T(1024)}, u32[]{:S(2)}) copy-start(f32[640]{0:T(1024)} %param.16) | copy-start | bytes 7684
  317.0 52.9 %copy-start.6 = (s32[4]{0:T(128)S(1)}, s32[4]{0:T(128)}, u32[]{:S(2)}) copy-start(s32[4]{0:T(128)} %param.12) | copy-start | bytes 52
  317.0 58.6 %copy-start.4 = (f32[640]{0:T(1024)S(1)}, f32[640]{0:T(1024)}, u32[]{:S(2)}) copy-start(f32[640]{0:T(1024)} %param.19) | copy-start | bytes 7684
  317.0 58.6 %copy-start.5 = (f32[640]{0:T(1024)S(1)}, f32[640]{0:T(1024)}, u32[]{:S(2)}) copy-start(f32[640]{0:T(1024)} %param.18) | copy-start | bytes 7684
  317.2 13.0 %collective-permute-start = (f32[184,640]{1,0:T(8,128)S(1)}, f32[184,640]{1,0:T(8,128)S(1)}, u32[]{:S(2)}, u32[]{:S(2)}) collective-permute-start(f32[184,640]{1,0:T(8,128)S(1)} %slice_select_fusion), channel_id=1, source_target_pairs={{0,16},{16,0},{32,48},{48,32},{64,80},{80,64},{96,112},{112,96},{1... | collective-permute-start | bytes 1413128 | tf_op jit(solution)/shard_map/ppermute | solution.py:46
  330.3 7.3 %collective-permute-start.1 = (f32[92,640]{1,0:T(8,128)S(1)}, f32[92,640]{1,0:T(8,128)S(1)}, u32[]{:S(2)}, u32[]{:S(2)}) collective-permute-start(f32[92,640]{1,0:T(8,128)S(1)} %slice_select_fusion.1), channel_id=1, source_target_pairs={{0,128},{16,144},{32,160},{48,176},{64,192},{80,208},{96,224},{112... | collective-permute-start | bytes 706568 | tf_op jit(solution)/shard_map/ppermute | solution.py:46
  337.8 7.4 %collective-permute-start.2 = (f32[46,640]{1,0:T(8,128)S(1)}, f32[46,640]{1,0:T(8,128)S(1)}, u32[]{:S(2)}, u32[]{:S(2)}) collective-permute-start(f32[46,640]{1,0:T(8,128)S(1)} %slice_select_fusion.2), channel_id=1, source_target_pairs={{0,32},{16,48},{32,0},{48,16},{64,96},{80,112},{96,64},{112,80},{1... | collective-permute-start | bytes 353288 | tf_op jit(solution)/shard_map/ppermute | solution.py:46
  345.2 8.2 %collective-permute-start.3 = (f32[23,640]{1,0:T(8,128)S(1)}, f32[23,640]{1,0:T(8,128)S(1)}, u32[]{:S(2)}, u32[]{:S(2)}) collective-permute-start(f32[23,640]{1,0:T(8,128)S(1)} %slice_select_fusion.3), channel_id=1, source_target_pairs={{0,64},{16,80},{32,96},{48,112},{64,0},{80,16},{96,32},{112,48},{1... | collective-permute-start | bytes 176648 | tf_op jit(solution)/shard_map/ppermute | solution.py:46
  353.4 8.5 %collective-permute-start.4 = (f32[23,640]{1,0:T(8,128)S(1)}, f32[23,640]{1,0:T(8,128)S(1)}, u32[]{:S(2)}, u32[]{:S(2)}) collective-permute-start(f32[23,640]{1,0:T(8,128)S(1)} %select_add_fusion.3), channel_id=1, source_target_pairs={{0,64},{16,80},{32,96},{48,112},{64,0},{80,16},{96,32},{112,48},{1... | collective-permute-start | bytes 176648 | tf_op jit(solution)/shard_map/ppermute | solution.py:50
  362.0 7.2 %collective-permute-start.5 = (f32[46,640]{1,0:T(8,128)S(1)}, f32[46,640]{1,0:T(8,128)S(1)}, u32[]{:S(2)}, u32[]{:S(2)}) collective-permute-start(f32[46,640]{1,0:T(8,128)S(1)} %maximum_select_fusion.3), channel_id=1, source_target_pairs={{0,32},{16,48},{32,0},{48,16},{64,96},{80,112},{96,64},{112,80},{1... | collective-permute-start | bytes 353288 | tf_op jit(solution)/shard_map/ppermute | solution.py:50
  369.2 6.3 %collective-permute-start.6 = (f32[92,640]{1,0:T(8,128)S(1)}, f32[92,640]{1,0:T(8,128)S(1)}, u32[]{:S(2)}, u32[]{:S(2)}) collective-permute-start(f32[92,640]{1,0:T(8,128)S(1)} %maximum_select_fusion.2), channel_id=1, source_target_pairs={{0,128},{16,144},{32,160},{48,176},{64,192},{80,208},{96,224},{112... | collective-permute-start | bytes 706568 | tf_op jit(solution)/shard_map/ppermute | solution.py:50
  375.6 13.4 %collective-permute-start.7 = (f32[184,640]{1,0:T(8,128)S(1)}, f32[184,640]{1,0:T(8,128)S(1)}, u32[]{:S(2)}, u32[]{:S(2)}) collective-permute-start(f32[184,640]{1,0:T(8,128)S(1)} %maximum_select_fusion.1), channel_id=1, source_target_pairs={{0,16},{16,0},{32,48},{48,32},{64,80},{80,64},{96,112},{112,96},{1... | collective-permute-start | bytes 1413128 | tf_op jit(solution)/shard_map/ppermute | solution.py:50
Sparse Core Ops, SparseCore 0:
  11.3 53.3 all-gather.8
  67.5 71.6 all-gather.6
  142.0 71.6 all-gather.4
  225.9 64.1 all-gather.10

commit v3 on v2

--- a/solution.py
+++ b/solution.py
@@ -52,6 +52,17 @@
     return cur[:rows]
 
 
+def doubling_sum(block, axis):
+    size = lax.axis_size(axis)
+    levels = size.bit_length() - 1
+    if size != 1 << levels:
+        return lax.psum(block, axis)
+    for level in range(levels):
+        pairs = [(i, i ^ (1 << level)) for i in range(size)]
+        block = block + lax.ppermute(block, axis, pairs)
+    return block
+
+
 def body(
     latents,
     bucket,
@@ -67,10 +78,6 @@
 ):
     slot_total, tile_side, _, channels = latents.shape
     row_block = conv_weight.shape[0]
-    conv_full = lax.all_gather(conv_weight, "fsdp", axis=0, tiled=True)
-    down_full = lax.all_gather(down_weight, "fsdp", axis=0, tiled=True)
-    conv_kernel = conv_full.reshape(3, 3, channels, channels)
-    down_kernel = down_full.reshape(3, 3, channels, channels)
 
     live = jnp.arange(slot_total, dtype=jnp.int32) < tile_count[0]
     live4 = live[:, None, None, None]
@@ -86,7 +93,18 @@
     pre_act = normed * norm_gain + norm_shift
     sigmoid_v = jax.nn.sigmoid(pre_act)
     activated = (pre_act * sigmoid_v).astype(jnp.bfloat16)
-    act_all = lax.all_gather(activated, "fsdp", axis=0, tiled=True)
+    cot_rows = masked_cot.reshape(-1, channels)
+    act_rows = activated.reshape(-1, channels)
+    sent = jnp.concatenate([conv_weight, down_weight, cot_rows, act_rows], axis=0)
+    got = lax.all_gather(sent, "fsdp", axis=0, tiled=False)
+    edges = [0]
+    for part in (conv_weight, down_weight, cot_rows, act_rows):
+        edges.append(edges[-1] + part.shape[0])
+    pieces = [got[:, edges[i] : edges[i + 1]] for i in range(4)]
+    conv_kernel = pieces[0].reshape(3, 3, channels, channels)
+    down_kernel = pieces[1].reshape(3, 3, channels, channels)
+    cot_all = pieces[2].reshape((-1,) + masked_cot.shape[1:])
+    act_all = pieces[3].reshape((-1,) + activated.shape[1:])
 
     conditioning = cond_table[bucket]
     conv_out = lax.conv_general_dilated(
@@ -110,7 +128,6 @@
     block_output = (down_out + down_bias).astype(jnp.bfloat16)
     block_output = jnp.where(live4, block_output, jnp.zeros_like(block_output))
 
-    cot_all = lax.all_gather(masked_cot, "fsdp", axis=0, tiled=True)
     resid_all = lax.conv_general_dilated(
         cot_all,
         down_kernel[::-1, ::-1],
@@ -147,7 +164,7 @@
             jnp.sum(grad_resid, axis=(0, 1, 2)),
         ]
     )
-    affine_fsdp = lax.psum(affine, "fsdp")
+    affine_fsdp = doubling_sum(affine, "fsdp")
 
     first_row = lax.axis_index("fsdp") * row_block
     first_tap = first_row // channels

time: 399 us -> 304 us (0.76)
  blocking collectives: 59.6 us -> 0 us
  waiting for transfers between devices: 228 us -> 171 us
  local copies, waits for them, and re-layouts: 23.8 us -> 35.3 us
  starting transfers between devices: 19.2 us -> 27.7 us
    psum x1 -> x0, blocking collectives: 59.6 us -> none  [body(): affine_fsdp = lax.psum(affine, 'fsdp')]
    all_gather x4 -> x1, waiting for transfers between devices: 188 us -> 137 us  [body(): got = lax.all_gather(sent, 'fsdp', axis=0, tiled=False)]
    slice x0 -> x3, local copies, waits for them, and re-layouts: none -> 14.8 us  [body(): pieces = [got[:, edges[i]:edges[i + 1]] for i in range(4)]]
    all_gather x1 -> x0, local copies, waits for them, and re-layouts: 7.88 us -> none  [body(): act_all = lax.all_gather(activated, 'fsdp', axis=0, tiled=True)]
    reshape x0 -> x3, local copies, waits for them, and re-layouts: none -> 5.77 us  [the longest x1 5.42 us: body(): act_all = pieces[3].reshape((-1,) + activated.shape[1:])]
    ppermute x0 -> x4, starting transfers between devices: none -> 4.04 us  [doubling_sum(): block = block + lax.ppermute(block, axis, pairs)]
  transfers between devices with their start and end apart: 12 -> 13, of which waited for: 11 -> 9; matrix products, arithmetic and copies ran while one was open for 8% -> 14% of each run, Pallas kernels for 0% -> 0%
where the time goes in v3:
time: 304 us; the launch traced here: 302 us
  waiting for transfers between devices  171 us (56%)
  matrix products  42.5 us (14%)
  local copies, waits for them, and re-layouts  35.3 us (12%)
  starting transfers between devices  27.7 us (9%)
  between operations  15.1 us (5%)
  other arithmetic  10.4 us (3%)
    all_gather x1, waiting for transfers between devices, body(): got = lax.all_gather(sent, 'fsdp', axis=0, tiled=False)  137 us
    ppermute x4, waiting for transfers between devices, halving_doubling_sum(): cur = keep + lax.ppermute(send, axis, pairs)  22.3 us
    conv_general_dilated x1, matrix products, body(): lax.conv_general_dilated(cot_all, down_kernel[::-1, ::-1], (1, 1), ((1, 2...  16.4 us
    slice x3, local copies, waits for them, and re-layouts, body(): pieces = [got[:, edges[i]:edges[i + 1]] for i in range(4)]  14.8 us
    ppermute x4, starting transfers between devices, halving_doubling_sum(): cur = keep + lax.ppermute(send, axis, pairs)  12 us
    conv_general_dilated x1, matrix products, body(): lax.conv_general_dilated(residual, down_kernel, (2, 2), ((1, 1), (1, 1)),...  11.9 us
    ppermute x4, starting transfers between devices, halving_doubling_sum(): other = lax.ppermute(cur, axis, pairs)  11.7 us
    ppermute x4, waiting for transfers between devices, halving_doubling_sum(): other = lax.ppermute(cur, axis, pairs)  10.1 us
  transfers between devices with their start and end apart: 13, of which 9 were waited for; matrix products, arithmetic and copies ran while one was open for 14% of the time, Pallas kernels for 0%

profile of v3, /device:TPU:2, one launch (start us, length us, event | category | flops | bytes accessed | tf_op | source)
XLA Modules:
  0.0 301.7 jit_solution(14087943777043307039)
XLA Ops:
  7.9 1.2 convert_reduce_fusion
  9.1 0.1 reshape.62
  9.4 0.1 sub.36
  9.6 1.3 fusion.30
  11.1 0.1 rsqrt.12
  11.3 1.0 copy_select_fusion
  12.3 1.6 multiply_convert_fusion
  13.9 2.4 pad_maximum_fusion
  16.4 137.4 %all-gather.3.cloned.1.call-done = bf16[16640,640]{1,0:T(8,128)(2,1)} async-done(((bf16[1040,640]{1,0:T(8,128)(2,1)}), bf16[16640,640]{1,0:T(8,128)(2,1)}) %all-gather.3.cloned.1.call-update) | async-done | bytes 21299216 | tf_op jit(solution)/shard_map/all_gather | solution.py:99
  153.7 1.4 slice.72
  155.2 10.5 %fusion.35 = (bf16[16,360,640]{2,1,0:T(8,128)(2,1)}, bf16[16,360,640]{2,1,0:T(8,128)(2,1)}) fusion(bf16[16,1040,640]{2,1,0:T(8,128)(2,1)} %bitcast.23), kind=kLoop, calls=%fused_computation.69 | loop fusion | bytes 29491200 | tf_op jit(solution)/shard_map/slice | solution.py:103
  165.7 0.3 reshape.68
  166.0 16.4 %fusion.9 = f32[64,8,8,640]{3,0,2,1:T(8,128)S(1)} fusion(bf16[3,3,640,640]{3,2,1,0:T(8,128)(2,1)} %bitcast.20, bf16[64,4,4,640]{3,2,1,0:T(4,128)(2,1)S(1)} %reshape.68), kind=kOutput, calls=%fused_computation.10 | convolution fusion | flops 6343884800 | bytes 19169280 | tf_op jit(solution)/shard_map/conv_general_dilated | solution.py:131
  182.5 4.7 %fusion.29 = (f32[640]{0:T(1024)S(1)}, f32[4,640]{1,0:T(4,128)S(1)}, f32[4,640]{1,0:T(4,128)S(1)}, f32[640]{0:T(1024)S(1)}, f32[4,8,8,640]{3,0,2,1:T(4,128)S(1)}) fusion(f32[4,640]{1,0:T(4,128)S(1)} %rsqrt.12, f32[4,640]{1,0:T(4,128)S(1)} %sub.36, bf16[4,8,8,640]{3,2,1,0:T(8,128)(2,1)S(1)} %copy-done.3, f32[640]{0:T(1024)S(1)} %copy-done.4, ...), kind=kOutput, calls=%fused_computation.38 | convolution fusion | flops 1589241600 | bytes 8737796 | tf_op jit(solution)/shard_map/conv_general_dilated | solution.py:145
  187.5 0.1 mul.83
  187.6 0.1 reshape.69
  187.9 0.1 sub.40
  188.1 2.0 dynamic-slice_reduce_fusion
  190.1 0.3 collective-permute-start
  190.5 0.9 collective-permute-done
  191.4 0.8 collective-permute-start.1
  192.2 2.9 slice.73
  195.2 5.4 %copy.24 = bf16[64,8,8,640]{3,0,2,1:T(8,128)(2,1)} copy(bf16[64,8,8,640]{3,2,1,0:T(8,128)(2,1)S(1)} %bitcast.25) | data formatting | bytes 10485760 | tf_op jit(solution)/shard_map/reshape | solution.py:107
  200.6 2.1 collective-permute-start.2
  202.7 9.7 %pad_dynamic-slice_fusion.2 = (bf16[64,8,8,640]{3,0,2,1:T(8,128)(2,1)}, bf16[64,8,8,640]{3,0,2,1:T(8,128)(2,1)}) fusion(s32[]{:T(128)S(6)} %select_n.145, s32[]{:T(128)S(6)} %select_n.147, bf16[64,8,8,640]{3,0,2,1:T(8,128)(2,1)} %copy.24, s32[]{:T(128)S(6)} %select_n.141, s32[]{:T(128)S(6)} %select_n.143), kind=kLoop, calls=%fused_computation.3 | loop fusion | bytes 15728656 | tf_op jit(solution)/shard_map/dynamic_slice | solution.py:23
  212.4 0.8 collective-permute-start.3
  213.2 9.5 %fusion.4 = f32[360,640]{1,0:T(8,128)S(1)} fusion(f32[64,8,8,640]{3,0,2,1:T(8,128)} %copy-done.1, s32[]{:T(128)S(6)} %select_n.149, bf16[64,8,8,640]{3,0,2,1:T(8,128)(2,1)} %get-tuple-element.21, bf16[64,8,8,640]{3,0,2,1:T(8,128)(2,1)} %get-tuple-element.20), kind=kOutput, calls=%fused_computation.8 | convolution fusion | flops 1895956480 | bytes 21893124 | tf_op jit(solution)/shard_map/dot_general | solution.py:179
  222.9 1.6 collective-permute-start.4
  224.6 10.5 %collective-permute-done.4 = f32[184,640]{1,0:T(8,128)S(1)} collective-permute-done((f32[184,640]{1,0:T(8,128)S(1)}, f32[184,640]{1,0:T(8,128)S(1)}, u32[]{:S(2)}, u32[]{:S(2)}) %collective-permute-start.4) | collective-permute-done | bytes 471072 | tf_op jit(solution)/shard_map/ppermute | solution.py:46
  235.2 1.6 collective-permute-start.5
  236.8 4.9 %collective-permute-done.5 = f32[92,640]{1,0:T(8,128)S(1)} collective-permute-done((f32[92,640]{1,0:T(8,128)S(1)}, f32[92,640]{1,0:T(8,128)S(1)}, u32[]{:S(2)}, u32[]{:S(2)}) %collective-permute-start.5) | collective-permute-done | bytes 235552 | tf_op jit(solution)/shard_map/ppermute | solution.py:46
  241.8 2.8 collective-permute-start.6
  244.6 4.6 %collective-permute-done.6 = f32[46,640]{1,0:T(8,128)S(1)} collective-permute-done((f32[46,640]{1,0:T(8,128)S(1)}, f32[46,640]{1,0:T(8,128)S(1)}, u32[]{:S(2)}, u32[]{:S(2)}) %collective-permute-start.6) | collective-permute-done | bytes 117792 | tf_op jit(solution)/shard_map/ppermute | solution.py:46
  249.2 5.9 %collective-permute-start.7 = (f32[23,640]{1,0:T(8,128)S(1)}, f32[23,640]{1,0:T(8,128)S(1)}, u32[]{:S(2)}, u32[]{:S(2)}) collective-permute-start(f32[23,640]{1,0:T(8,128)S(1)} %slice_select_fusion.3), channel_id=1, source_target_pairs={{0,64},{16,80},{32,96},{48,112},{64,0},{80,16},{96,32},{112,48},{1... | collective-permute-start | bytes 176648 | tf_op jit(solution)/shard_map/ppermute | solution.py:46
  255.1 2.3 collective-permute-done.7
  257.4 6.0 %collective-permute-start.8 = (f32[23,640]{1,0:T(8,128)S(1)}, f32[23,640]{1,0:T(8,128)S(1)}, u32[]{:S(2)}, u32[]{:S(2)}) collective-permute-start(f32[23,640]{1,0:T(8,128)S(1)} %select_add_fusion.3), channel_id=1, source_target_pairs={{0,64},{16,80},{32,96},{48,112},{64,0},{80,16},{96,32},{112,48},{1... | collective-permute-start | bytes 176648 | tf_op jit(solution)/shard_map/ppermute | solution.py:50
  263.4 2.2 collective-permute-done.8
  265.7 1.6 collective-permute-start.9
  267.3 4.3 %collective-permute-done.9 = f32[46,640]{1,0:T(8,128)S(1)} collective-permute-done((f32[46,640]{1,0:T(8,128)S(1)}, f32[46,640]{1,0:T(8,128)S(1)}, u32[]{:S(2)}, u32[]{:S(2)}) %collective-permute-start.9) | collective-permute-done | bytes 117792 | tf_op jit(solution)/shard_map/ppermute | solution.py:50
  271.6 2.9 collective-permute-start.10
  274.5 0.6 gather_fusion
  275.1 3.6 %collective-permute-done.10 = f32[92,640]{1,0:T(8,128)S(1)} collective-permute-done((f32[92,640]{1,0:T(8,128)S(1)}, f32[92,640]{1,0:T(8,128)S(1)}, u32[]{:S(2)}, u32[]{:S(2)}) %collective-permute-start.10) | collective-permute-done | bytes 235552 | tf_op jit(solution)/shard_map/ppermute | solution.py:50
  278.7 1.2 collective-permute-start.11
  279.9 11.9 %fusion.16 = bf16[4,4,4,640]{3,0,2,1:T(4,128)(2,1)S(1)} fusion(bf16[3,3,640,640]{3,2,1,0:T(8,128)(2,1)} %bitcast.21, f32[640]{0:T(1024)S(1)} %copy-done.6, pred[4]{0:T(512)(128)(4,1)S(1)} %iota_compare_fusion, bf16[3,3,640,640]{3,2,1,0:T(8,128)(2,1)} %bitcast.26, f32[4,640]{1,0:T(4,128)S(1)} %gather_fusion, f32[640]{0:T(1024)S(1)} %copy-done.7, ...), kind=kOutput, calls=%fused_computation.20 | convolution fusion | flops 1985044480 | bytes 15196164 | tf_op jit(solution)/shard_map/conv_general_dilated | solution.py:120
  291.8 0.7 copy.25
  292.5 0.8 copy.26
  293.3 0.6 slice.82
  293.9 1.0 slice.81
  (65 shorter events, 1.7 us)
Async XLA Ops:
  7.2 267.3 %copy-start = (f32[40,640]{1,0:T(8,128)S(1)}, f32[40,640]{1,0:T(8,128)}, u32[]{:S(2)}) copy-start(f32[40,640]{1,0:T(8,128)} %param.15) | copy-start | bytes 307204
  7.2 146.6 %all-gather.3.cloned.1.call-start = ((), (), s32[]{:S(2)}) async-start(), calls=%async_computation | async-start | bytes 22630400 | tf_op jit(solution)/shard_map/all_gather | solution.py:99
  166.0 16.5 %copy-start.2 = (bf16[16,360,640]{2,1,0:T(8,128)(2,1)S(1)}, bf16[16,360,640]{2,1,0:T(8,128)(2,1)}, u32[]{:S(2)}) copy-start(bf16[16,360,640]{2,1,0:T(8,128)(2,1)} %get-tuple-element.17) | copy-start | bytes 22118404
  166.0 16.5 %copy-start.3 = (bf16[4,8,8,640]{3,2,1,0:T(8,128)(2,1)S(1)}, bf16[4,8,8,640]{3,2,1,0:T(8,128)(2,1)}, u32[]{:S(2)}) copy-start(bf16[4,8,8,640]{3,2,1,0:T(8,128)(2,1)} %param.11) | copy-start | bytes 983044
  166.0 16.4 %copy-start.4 = (f32[640]{0:T(1024)S(1)}, f32[640]{0:T(1024)}, u32[]{:S(2)}) copy-start(f32[640]{0:T(1024)} %param.16) | copy-start | bytes 7684
  166.0 16.4 %copy-start.5 = (f32[640]{0:T(1024)S(1)}, f32[640]{0:T(1024)}, u32[]{:S(2)}) copy-start(f32[640]{0:T(1024)} %param.17) | copy-start | bytes 7684
  182.4 4.8 %copy-start.1 = (f32[64,8,8,640]{3,0,2,1:T(8,128)}, f32[64,8,8,640]{3,0,2,1:T(8,128)S(1)}, u32[]{:S(2)}) copy-start(f32[64,8,8,640]{3,0,2,1:T(8,128)S(1)} %fusion.9) | copy-start | bytes 31457284
  190.1 1.3 collective-permute-start
  191.4 9.2 %collective-permute-start.1 = (f32[3,640]{1,0:T(4,128)S(1)}, f32[3,640]{1,0:T(4,128)S(1)}, u32[]{:S(2)}, u32[]{:S(2)}) collective-permute-start(f32[3,640]{1,0:T(4,128)S(1)} %fusion.34), channel_id=1, source_target_pairs={{0,2},{1,3},{2,0},{3,1},{4,6},{5,7},{6,4},{7,5},{8,10},{9,11},{10,... | collective-permute-start | bytes 23048 | tf_op jit(solution)/shard_map/ppermute | solution.py:62
  200.6 11.8 %collective-permute-start.2 = (f32[3,640]{1,0:T(4,128)S(1)}, f32[3,640]{1,0:T(4,128)S(1)}, u32[]{:S(2)}, u32[]{:S(2)}) collective-permute-start(f32[3,640]{1,0:T(4,128)S(1)} %fusion.41), channel_id=1, source_target_pairs={{0,4},{1,5},{2,6},{3,7},{4,0},{5,1},{6,2},{7,3},{8,12},{9,13},{10,... | collective-permute-start | bytes 23048 | tf_op jit(solution)/shard_map/ppermute | solution.py:62
  212.4 10.4 %collective-permute-start.3 = (f32[3,640]{1,0:T(4,128)S(1)}, f32[3,640]{1,0:T(4,128)S(1)}, u32[]{:S(2)}, u32[]{:S(2)}) collective-permute-start(f32[3,640]{1,0:T(4,128)S(1)} %add.148), channel_id=1, source_target_pairs={{0,8},{1,9},{2,10},{3,11},{4,12},{5,13},{6,14},{7,15},{8,0},{9,1},... | collective-permute-start | bytes 23048 | tf_op jit(solution)/shard_map/ppermute | solution.py:62
  222.7 51.7 %copy-start.8 = (s32[4]{0:T(128)S(1)}, s32[4]{0:T(128)}, u32[]{:S(2)}) copy-start(s32[4]{0:T(128)} %param.12) | copy-start | bytes 52
  222.8 57.1 %copy-start.6 = (f32[640]{0:T(1024)S(1)}, f32[640]{0:T(1024)}, u32[]{:S(2)}) copy-start(f32[640]{0:T(1024)} %param.19) | copy-start | bytes 7684
  222.8 57.1 %copy-start.7 = (f32[640]{0:T(1024)S(1)}, f32[640]{0:T(1024)}, u32[]{:S(2)}) copy-start(f32[640]{0:T(1024)} %param.18) | copy-start | bytes 7684
  222.9 12.2 %collective-permute-start.4 = (f32[184,640]{1,0:T(8,128)S(1)}, f32[184,640]{1,0:T(8,128)S(1)}, u32[]{:S(2)}, u32[]{:S(2)}) collective-permute-start(f32[184,640]{1,0:T(8,128)S(1)} %slice_select_fusion), channel_id=1, source_target_pairs={{0,16},{16,0},{32,48},{48,32},{64,80},{80,64},{96,112},{112,96},{1... | collective-permute-start | bytes 1413128 | tf_op jit(solution)/shard_map/ppermute | solution.py:46
  235.2 6.5 %collective-permute-start.5 = (f32[92,640]{1,0:T(8,128)S(1)}, f32[92,640]{1,0:T(8,128)S(1)}, u32[]{:S(2)}, u32[]{:S(2)}) collective-permute-start(f32[92,640]{1,0:T(8,128)S(1)} %slice_select_fusion.1), channel_id=1, source_target_pairs={{0,128},{16,144},{32,160},{48,176},{64,192},{80,208},{96,224},{112... | collective-permute-start | bytes 706568 | tf_op jit(solution)/shard_map/ppermute | solution.py:46
  241.8 7.4 %collective-permute-start.6 = (f32[46,640]{1,0:T(8,128)S(1)}, f32[46,640]{1,0:T(8,128)S(1)}, u32[]{:S(2)}, u32[]{:S(2)}) collective-permute-start(f32[46,640]{1,0:T(8,128)S(1)} %slice_select_fusion.2), channel_id=1, source_target_pairs={{0,32},{16,48},{32,0},{48,16},{64,96},{80,112},{96,64},{112,80},{1... | collective-permute-start | bytes 353288 | tf_op jit(solution)/shard_map/ppermute | solution.py:46
  249.2 8.2 %collective-permute-start.7 = (f32[23,640]{1,0:T(8,128)S(1)}, f32[23,640]{1,0:T(8,128)S(1)}, u32[]{:S(2)}, u32[]{:S(2)}) collective-permute-start(f32[23,640]{1,0:T(8,128)S(1)} %slice_select_fusion.3), channel_id=1, source_target_pairs={{0,64},{16,80},{32,96},{48,112},{64,0},{80,16},{96,32},{112,48},{1... | collective-permute-start | bytes 176648 | tf_op jit(solution)/shard_map/ppermute | solution.py:46
  257.4 8.2 %collective-permute-start.8 = (f32[23,640]{1,0:T(8,128)S(1)}, f32[23,640]{1,0:T(8,128)S(1)}, u32[]{:S(2)}, u32[]{:S(2)}) collective-permute-start(f32[23,640]{1,0:T(8,128)S(1)} %select_add_fusion.3), channel_id=1, source_target_pairs={{0,64},{16,80},{32,96},{48,112},{64,0},{80,16},{96,32},{112,48},{1... | collective-permute-start | bytes 176648 | tf_op jit(solution)/shard_map/ppermute | solution.py:50
  265.7 5.9 %collective-permute-start.9 = (f32[46,640]{1,0:T(8,128)S(1)}, f32[46,640]{1,0:T(8,128)S(1)}, u32[]{:S(2)}, u32[]{:S(2)}) collective-permute-start(f32[46,640]{1,0:T(8,128)S(1)} %maximum_select_fusion.3), channel_id=1, source_target_pairs={{0,32},{16,48},{32,0},{48,16},{64,96},{80,112},{96,64},{112,80},{1... | collective-permute-start | bytes 353288 | tf_op jit(solution)/shard_map/ppermute | solution.py:50
  271.6 7.1 %collective-permute-start.10 = (f32[92,640]{1,0:T(8,128)S(1)}, f32[92,640]{1,0:T(8,128)S(1)}, u32[]{:S(2)}, u32[]{:S(2)}) collective-permute-start(f32[92,640]{1,0:T(8,128)S(1)} %maximum_select_fusion.2), channel_id=1, source_target_pairs={{0,128},{16,144},{32,160},{48,176},{64,192},{80,208},{96,224},{112... | collective-permute-start | bytes 706568 | tf_op jit(solution)/shard_map/ppermute | solution.py:50
  278.7 14.5 %collective-permute-start.11 = (f32[184,640]{1,0:T(8,128)S(1)}, f32[184,640]{1,0:T(8,128)S(1)}, u32[]{:S(2)}, u32[]{:S(2)}) collective-permute-start(f32[184,640]{1,0:T(8,128)S(1)} %maximum_select_fusion.1), channel_id=1, source_target_pairs={{0,16},{16,0},{32,48},{48,32},{64,80},{80,64},{96,112},{112,96},{1... | collective-permute-start | bytes 1413128 | tf_op jit(solution)/shard_map/ppermute | solution.py:50
Sparse Core Ops, SparseCore 0:
  16.5 137.2 all-gather.2
